TPU v7x, 32 devices: a whole 2x2x4 slice. The times are simulated.
32 devices in a mesh: days: 2 (over y), chan: 4 (over z), win: 4 (over x, core).
Axes of the slice: x: 2, y: 2, z: 4, core: 2. Of those that a mesh axis runs over, the one named last changes fastest.
Arguments:
- spectra: bfloat16 [2560, 32, 1024], P(('days', 'chan'), 'win'), parts along dimension 0, may hold values from -17 to 17
- pair_anchor: int32 [2048], P('chan'), may hold values from 0 to 319
- pair_offset: int32 [2048], P('chan'), may hold values from 0 to 2
- pair_partner: int32 [2048], P('chan'), may hold values from 0 to 319
- pair_count: int32 [4], P('chan'), may hold values from 1 to 512, as said below
- window_bins: int32 [64], P(('days', 'win')), parts along dimension 0, may hold values from 0 to 7
- bin_gain: float32 [8], replicated, may hold values from 0.2 to 5
Outputs:
- ref_stack: float32 [4096, 128], P(('days', 'chan')), parts along dimension 0
- restack: float32 [4096, 128], P(('days', 'chan')), parts along dimension 0
There are 2 independent parts, one for each index of `days`. A program takes and returns all parts, laid end to end along the dimension named above; an argument that names none is the same for every part. Nothing has to cross between parts.
Inputs may be any that keep to these rules, and one draw needn't show every extreme that they name: `pair_count`: each block holds from 1 to 512 live pair slots, the first ones of its slots; some block holds 512 in every draw.
All inputs are finite; a program needn't handle non-finite values.
Results may differ from a plain program's by a relative error of at most 0.0062.
Values may be sent and summed in bfloat16 or wider, within the bound.
No kernel may reach another device: no remote copies, remote signals or barrier semaphores. Data moves between devices by JAX's collectives and lax.ppermute only.
A program may use at most 128 MiB of HBM per device.

v0:
```python
import jax
import jax.numpy as jnp
from jax import lax
from jax.sharding import PartitionSpec as P

LAG = 128
EPS_POWER = 1e-05
EPS_LAG = 1e-06


def ring_neighbours(shard, axis):
    peers = lax.axis_size(axis)
    up = [(i, (i + 1) % peers) for i in range(peers)]
    down = [(j, i) for i, j in up]
    before = lax.ppermute(shard, axis, up)
    after = lax.ppermute(shard, axis, down)
    return (before, after)


def whiten(spectra):
    spectra_f = spectra.astype(jnp.float32)
    power_mean = jnp.mean(spectra_f * spectra_f, axis=-1, keepdims=True)
    return (spectra_f * lax.rsqrt(power_mean + EPS_POWER)).astype(jnp.bfloat16)


def lag_table(freq_count, lag_count):
    freq_ids = lax.broadcasted_iota(jnp.float32, (freq_count, lag_count), 0)
    lag_ids = lax.broadcasted_iota(jnp.float32, (freq_count, lag_count), 1) - lag_count // 2
    angles = 2.0 * jnp.pi / (2 * freq_count) * freq_ids * lag_ids
    norm_scale = 1.0 / jnp.sqrt(jnp.float32(freq_count))
    return jnp.concatenate(
        [jnp.cos(angles) * norm_scale, -jnp.sin(angles) * norm_scale], axis=0
    ).astype(jnp.bfloat16)


def cross_spectra(anchors, partners):
    half_width = anchors.shape[-1] // 2
    anchor_f = anchors.astype(jnp.float32)
    partner_f = partners.astype(jnp.float32)
    anchor_re = anchor_f[..., :half_width]
    anchor_im = anchor_f[..., half_width:]
    partner_re = partner_f[..., :half_width]
    partner_im = partner_f[..., half_width:]
    cross_re = anchor_re * partner_re + anchor_im * partner_im
    cross_im = anchor_im * partner_re - anchor_re * partner_im
    return jnp.concatenate([cross_re, cross_im], axis=-1).astype(jnp.bfloat16)


def window_gains(bins, gains):
    levels = lax.broadcasted_iota(jnp.int32, (bins.shape[0], gains.shape[0]), 1)
    return jnp.sum(jnp.where(bins[:, None] == levels, gains[None, :], jnp.float32(0.0)), axis=1)


def window_weights(lag_corr, ref_sum, window_gain):
    corr_f = lag_corr.astype(jnp.float32)
    inner_prod = jnp.mean(corr_f * ref_sum[:, None, :], axis=-1)
    corr_rms = jnp.sqrt(jnp.mean(corr_f * corr_f, axis=-1) + EPS_LAG)
    ref_rms = jnp.sqrt(jnp.mean(ref_sum * ref_sum, axis=-1) + EPS_LAG)
    coherence = inner_prod / (corr_rms * ref_rms[:, None])
    weights = window_gain[None, :] * jnp.exp(2.0 * coherence)
    numerator = jnp.sum(weights[:, :, None] * corr_f, axis=1)
    denominator = jnp.sum(weights, axis=1)
    return (numerator, denominator)


def select_rows(selector, rows):
    return jnp.einsum("sc,cwf->swf", selector, rows, preferred_element_type=jnp.float32)


def local(spectra, pair_anchor, pair_offset, pair_partner, pair_count, window_bins, bin_gain):
    block_chans, local_wins, spec_width = spectra.shape
    pair_slots = pair_anchor.shape[0]
    white = whiten(spectra)
    before, after = ring_neighbours(white, "chan")
    transform = lag_table(spec_width // 2, LAG)
    lag_count = transform.shape[1]
    live_count = pair_count[0]
    chan_ids = lax.broadcasted_iota(jnp.int32, (pair_slots, block_chans), 1)
    pick_anchor = (pair_anchor[:, None] == chan_ids).astype(jnp.bfloat16)
    pick_partner = pair_partner[:, None] == chan_ids
    offsets = pair_offset[:, None]
    anchors = select_rows(pick_anchor, white).astype(jnp.bfloat16)
    partners = (
        select_rows((pick_partner & (offsets == 1)).astype(jnp.bfloat16), white)
        + select_rows((pick_partner & (offsets == 0)).astype(jnp.bfloat16), before)
        + select_rows((pick_partner & (offsets == 2)).astype(jnp.bfloat16), after)
    ).astype(jnp.bfloat16)
    cross_spec = cross_spectra(anchors, partners)
    corr_full = jnp.dot(
        cross_spec.reshape(pair_slots * local_wins, spec_width),
        transform,
        preferred_element_type=jnp.float32,
    ).reshape(pair_slots, local_wins, lag_count)
    corr_all = corr_full.astype(jnp.bfloat16)
    running = jnp.sum(corr_full, axis=1)
    ref_sum = lax.psum(running, "win")
    norm_scale = jnp.sqrt(jnp.float32(local_wins * lax.axis_size("win")))
    slot_ids = lax.broadcasted_iota(jnp.int32, (pair_slots,), 0)
    live = slot_ids < live_count
    ref_stack = jnp.where(live[:, None], ref_sum / norm_scale, 0.0)
    window_gain = window_gains(window_bins, bin_gain)
    numerator, denominator = window_weights(corr_all, ref_sum, window_gain)
    numerator, denominator = lax.psum((numerator, denominator), "win")
    restack = jnp.where(live[:, None], norm_scale * numerator / denominator[:, None], 0.0)
    return (ref_stack, restack)


def solution(mesh):
    in_specs = (
        P(("days", "chan"), "win", None),
        P("chan"),
        P("chan"),
        P("chan"),
        P("chan"),
        P(("days", "win")),
        P(),
    )
    out_specs = (P(("days", "chan"), None), P(("days", "chan"), None))
    return jax.shard_map(local, mesh=mesh, in_specs=in_specs, out_specs=out_specs, check_vma=False)
```

profile of v0, /device:TPU:0, one launch (start us, length us, event | category | flops | bytes accessed | tf_op | source)
XLA Modules:
  0.0 373.9 jit_solution(18302945717183395102)
XLA Ops:
  7.2 0.0 copy-start.4
  7.2 0.0 copy-start.3
  7.2 0.0 all-reduce.3.cloned.1.call-start
  7.2 0.0 copy-start
  7.2 8.1 %fusion = f32[320,8]{0,1:T(8,128)S(1)} fusion(bf16[320,8,1024]{2,1,0:T(8,128)(2,1)} %param.7), kind=kLoop, calls=%fused_computation.3 | loop fusion | flops 7861760 | bytes 5253120 | tf_op jit(solution)/shard_map/reduce_sum | solution.py:22
  15.4 0.0 copy-done
  15.4 4.2 %fusion.1 = bf16[320,8,1024]{2,0,1:T(8,128)(2,1)S(1)} fusion(f32[320,8]{0,1:T(8,128)S(1)} %add_rsqrt_fusion, bf16[320,8,1024]{2,1,0:T(8,128)(2,1)S(1)} %copy-done), kind=kLoop, calls=%fused_computation.4 | loop fusion | flops 7864320 | bytes 10496000 | tf_op jit(solution)/shard_map/convert_element_type | solution.py:23
  19.5 3.1 collective-permute-start
  22.6 2.3 collective-permute-start.1
  25.6 0.0 copy-done.4
  25.6 1.1 fusion.31
  26.7 0.0 copy-done.3
  26.7 0.0 copy-start.2
  26.7 8.2 %convert_convert_fusion = f32[512,8,1024]{2,0,1:T(8,128)} fusion(bf16[320,8,1024]{2,0,1:T(8,128)(2,1)S(1)} %fusion.1, s32[512]{0:T(512)S(1)} %copy-done.3), kind=kOutput, calls=%fused_computation.11 | convolution fusion | flops 2692907008 | bytes 22022144 | tf_op jit(solution)/shard_map/sc,cwf->swf/dot_general | solution.py:67
  35.0 0.0 copy-done.2
  35.0 8.2 %fusion.16 = f32[512,8,1024]{2,0,1:T(8,128)} fusion(bf16[320,8,1024]{2,0,1:T(8,128)(2,1)S(1)} %fusion.1, s32[512]{0:T(512)S(1)} %copy-done.2, pred[512]{0:T(512)(128)(4,1)S(1)} %get-tuple-element.17), kind=kOutput, calls=%fused_computation.26 | convolution fusion | flops 2684682240 | bytes 22022656 | tf_op jit(solution)/shard_map/sc,cwf->swf/dot_general | solution.py:67
  43.2 95.4 %collective-permute-done = bf16[320,8,1024]{2,0,1:T(8,128)(2,1)S(1)} collective-permute-done((bf16[320,8,1024]{2,0,1:T(8,128)(2,1)S(1)}, bf16[320,8,1024]{2,0,1:T(8,128)(2,1)S(1)}, u32[]{:S(2)}, u32[]{:S(2)}) %collective-permute-start) | collective-permute-done | bytes 5242912 | tf_op jit(solution)/shard_map/ppermute | solution.py:15
  138.6 8.2 %fusion.19 = f32[512,8,1024]{2,0,1:T(8,128)} fusion(bf16[320,8,1024]{2,0,1:T(8,128)(2,1)S(1)} %collective-permute-done, s32[512]{0:T(512)S(1)} %copy-done.2, pred[512]{0:T(512)(128)(4,1)S(1)} %get-tuple-element.18), kind=kOutput, calls=%fused_computation.28 | convolution fusion | flops 2684682240 | bytes 22022656 | tf_op jit(solution)/shard_map/sc,cwf->swf/dot_general | solution.py:67
  146.7 102.7 %collective-permute-done.1 = bf16[320,8,1024]{2,0,1:T(8,128)(2,1)S(1)} collective-permute-done((bf16[320,8,1024]{2,0,1:T(8,128)(2,1)S(1)}, bf16[320,8,1024]{2,0,1:T(8,128)(2,1)S(1)}, u32[]{:S(2)}, u32[]{:S(2)}) %collective-permute-start.1) | collective-permute-done | bytes 5242912 | tf_op jit(solution)/shard_map/ppermute | solution.py:16
  249.5 0.0 copy-start.1
  249.5 2.4 copy-done.1
  251.9 20.8 %fusion.6 = f32[512,8,1024]{2,0,1:T(8,128)} fusion(bf16[320,8,1024]{2,0,1:T(8,128)(2,1)} %copy-done.1, f32[512,8,1024]{2,0,1:T(8,128)} %fusion.16, f32[512,8,1024]{2,0,1:T(8,128)} %fusion.19, s32[512]{0:T(512)S(1)} %copy-done.2, pred[512]{0:T(512)(128)(4,1)S(1)} %get-tuple-element.16), kind=kOutput, calls=%fused_computation.12 | convolution fusion | flops 2701459456 | bytes 55577088 | tf_op jit(solution)/shard_map/sc,cwf->swf/dot_general | solution.py:67
  272.6 13.0 %add_convert_fusion.1 = (bf16[512,8,512]{2,0,1:T(8,128)(2,1)S(1)}, bf16[512,8,512]{2,0,1:T(8,128)(2,1)S(1)}) fusion(f32[512,8,1024]{2,0,1:T(8,128)} %fusion.6, f32[512,8,1024]{2,0,1:T(8,128)} %convert_convert_fusion), kind=kLoop, calls=%fused_computation.10 | loop fusion | flops 16777216 | bytes 41943040 | tf_op jit(solution)/shard_map/convert.2
  285.7 0.0 copy-start.5
  285.7 0.0 copy-start.6
  285.7 3.7 %fusion.39 = (f32[512,128]{0,1:T(8,128)}, bf16[512,8,128]{0,2,1:T(8,128)(2,1)S(1)}) fusion(bf16[512,128]{0,1:T(8,128)(2,1)S(1)} %get-tuple-element.15, bf16[512,128]{0,1:T(8,128)(2,1)S(1)} %get-tuple-element.14, bf16[512,8,512]{2,0,1:T(8,128)(2,1)S(1)} %get-tuple-element.11, bf16[512,8,512]{2,0,1:T(8,128)(2,1)S(1)} %get-tuple-element.10), kind=kOutput, calls=%fused_computation.63 | convolution fusion | flops 1092026368 | bytes 9961472 | tf_op jit(solution)/shard_map/dot_general | solution.py:89
  289.5 0.0 all-reduce.3.cloned.1.call-update
  289.5 0.0 all-reduce.5.cloned.1.call-start
  289.5 0.0 copy-done.5
  289.6 0.0 copy-done.6
  289.6 0.2 select_reduce_fusion
  289.7 40.0 %all-reduce.3.cloned.1.call-done = f32[512,128]{0,1:T(8,128)} async-done(((f32[512,128]{0,1:T(8,128)}), f32[512,128]{0,1:T(8,128)}) %all-reduce.3.cloned.1.call-update) | async-done | bytes 262160 | tf_op jit(solution)/shard_map/psum | solution.py:96
  329.7 1.0 multiply_reduce_fusion
  330.8 1.4 fusion.7
  332.1 0.1 fusion.38
  332.2 0.9 fusion.9
  333.1 0.0 all-reduce.5.cloned.1.call-update
  333.1 0.8 copy.15
  334.0 5.7 %psum.23 = f32[512]{0:T(512)S(1)} all-reduce(f32[512]{0:T(512)S(1)} %get-tuple-element.8), channel_id=1, replica_groups=mesh['days'=2,'chan'=4,'win'=4] {'win'}, use_global_device_ids=true, to_apply=%region_10.11 | all-reduce | flops 512 | bytes 4096 | tf_op jit(solution)/shard_map/psum | solution.py:103
  339.7 25.6 %all-reduce.5.cloned.1.call-done = f32[512,128]{0,1:T(8,128)} async-done(((f32[512,128]{0,1:T(8,128)}), f32[512,128]{0,1:T(8,128)}) %all-reduce.5.cloned.1.call-update) | async-done | bytes 262160 | tf_op jit(solution)/shard_map/psum | solution.py:103
  365.3 1.0 divide_select_fusion
  366.3 0.8 copy.16
  (6 shorter events, 0.0 us)
Async XLA Ops:
  7.2 18.4 %copy-start.4 = (s32[512]{0:T(512)S(1)}, s32[512]{0:T(512)}, u32[]{:S(2)}) copy-start(s32[512]{0:T(512)} %param.9) | copy-start | bytes 6148
  7.2 19.6 %copy-start.3 = (s32[512]{0:T(512)S(1)}, s32[512]{0:T(512)}, u32[]{:S(2)}) copy-start(s32[512]{0:T(512)} %param.8) | copy-start | bytes 6148
  7.2 322.6 %all-reduce.3.cloned.1.call-start = ((), (), s32[]{:S(2)}) async-start(), calls=%async_computation | async-start | bytes 524288 | tf_op jit(solution)/shard_map/psum | solution.py:96
  7.2 8.1 %copy-start = (bf16[320,8,1024]{2,1,0:T(8,128)(2,1)S(1)}, bf16[320,8,1024]{2,1,0:T(8,128)(2,1)}, u32[]{:S(2)}) copy-start(bf16[320,8,1024]{2,1,0:T(8,128)(2,1)} %param.7) | copy-start | bytes 15728644
  19.5 119.0 %collective-permute-start = (bf16[320,8,1024]{2,0,1:T(8,128)(2,1)S(1)}, bf16[320,8,1024]{2,0,1:T(8,128)(2,1)S(1)}, u32[]{:S(2)}, u32[]{:S(2)}) collective-permute-start(bf16[320,8,1024]{2,0,1:T(8,128)(2,1)S(1)} %fusion.1), channel_id=1, source_target_pairs={{0,4},{4,8},{8,12},{12,0},{1,5},{5,9},{9,13},{13,1},{2,6},{6,10},{... | collective-permute-start | bytes 15728648 | tf_op jit(solution)/shard_map/ppermute | solution.py:15
  22.6 226.9 %collective-permute-start.1 = (bf16[320,8,1024]{2,0,1:T(8,128)(2,1)S(1)}, bf16[320,8,1024]{2,0,1:T(8,128)(2,1)S(1)}, u32[]{:S(2)}, u32[]{:S(2)}) collective-permute-start(bf16[320,8,1024]{2,0,1:T(8,128)(2,1)S(1)} %fusion.1), channel_id=1, source_target_pairs={{4,0},{8,4},{12,8},{0,12},{5,1},{9,5},{13,9},{1,13},{6,2},{10,6},{... | collective-permute-start | bytes 15728648 | tf_op jit(solution)/shard_map/ppermute | solution.py:16
  26.7 8.2 %copy-start.2 = (s32[512]{0:T(512)S(1)}, s32[512]{0:T(512)}, u32[]{:S(2)}) copy-start(s32[512]{0:T(512)} %param.10) | copy-start | bytes 6148
  249.5 2.4 copy-start.1
  285.7 3.9 %copy-start.5 = (f32[8]{0:T(128)S(1)}, f32[8]{0:T(128)}, u32[]{:S(2)}) copy-start(f32[8]{0:T(128)} %param.13) | copy-start | bytes 100
  285.7 3.9 %copy-start.6 = (s32[8]{0:T(128)S(1)}, s32[8]{0:T(128)}, u32[]{:S(2)}) copy-start(s32[8]{0:T(128)} %param.12) | copy-start | bytes 100
  289.5 75.8 %all-reduce.5.cloned.1.call-start = ((), (), s32[]{:S(2)}) async-start(), calls=%async_computation.1 | async-start | bytes 524288 | tf_op jit(solution)/shard_map/psum | solution.py:103
Sparse Core Ops, SparseCore 0:
  289.6 40.0 all-reduce.2
  333.3 31.9 all-reduce.4
where the time goes:
time: 374 us
  waiting for transfers between devices  264 us (71%)
  matrix products  49.1 us (13%)
  other arithmetic  31 us (8%)
  between operations  14.8 us (4%)
  blocking collectives  5.73 us (2%)
  starting transfers between devices  5.43 us (1%)
  local copies, waits for them, and re-layouts  4.09 us (1%)
    ppermute x1, waiting for transfers between devices, ring_neighbours(): after = lax.ppermute(shard, axis, down)  103 us
    ppermute x1, waiting for transfers between devices, ring_neighbours(): before = lax.ppermute(shard, axis, up)  95.4 us
    dot_general x4, matrix products, select_rows(): jnp.einsum('sc,cwf->swf', selector, rows, preferred_element_type=jnp.floa...  45.4 us
    psum x1, waiting for transfers between devices, local(): ref_sum = lax.psum(running, 'win')  40 us
    psum x1, waiting for transfers between devices, local(): numerator, denominator = lax.psum((numerator, denominator), 'win')  25.6 us
    another operation x2, other arithmetic  14.2 us
    reduce_sum x1, other arithmetic, whiten(): power_mean = jnp.mean(spectra_f * spectra_f, axis=-1, keepdims=True)  8.1 us
  transfers between devices with their start and end apart: 4, of which 4 were waited for; matrix products, arithmetic and copies ran while one was open for 7% of the time, Pallas kernels for 0%

commit v1 on v0

--- a/solution.py
+++ b/solution.py
@@ -93,7 +93,7 @@
     ).reshape(pair_slots, local_wins, lag_count)
     corr_all = corr_full.astype(jnp.bfloat16)
     running = jnp.sum(corr_full, axis=1)
-    ref_sum = lax.psum(running, "win")
+    ref_sum = jnp.sum(lax.all_gather(running, "win"), axis=0)
     norm_scale = jnp.sqrt(jnp.float32(local_wins * lax.axis_size("win")))
     slot_ids = lax.broadcasted_iota(jnp.int32, (pair_slots,), 0)
     live = slot_ids < live_count

time: 374 us -> 360 us (0.963)
  waiting for transfers between devices: 264 us -> 248 us
    psum x1 -> x0, waiting for transfers between devices: 40 us -> none  [local(): ref_sum = lax.psum(running, 'win')]
    all_gather x0 -> x1, waiting for transfers between devices: none -> 24.1 us  [local(): ref_sum = jnp.sum(lax.all_gather(running, 'win'), axis=0)]
where the time goes in v1:
time: 360 us; the launch traced here: 359 us
  waiting for transfers between devices  248 us (69%)
  matrix products  49.1 us (14%)
  other arithmetic  29.7 us (8%)
  between operations  14.8 us (4%)
  local copies, waits for them, and re-layouts  6.02 us (2%)
  blocking collectives  5.86 us (2%)
  starting transfers between devices  5.43 us (2%)
    ppermute x1, waiting for transfers between devices, ring_neighbours(): after = lax.ppermute(shard, axis, down)  103 us
    ppermute x1, waiting for transfers between devices, ring_neighbours(): before = lax.ppermute(shard, axis, up)  96 us
    dot_general x4, matrix products, select_rows(): jnp.einsum('sc,cwf->swf', selector, rows, preferred_element_type=jnp.floa...  45.4 us
    psum x1, waiting for transfers between devices, local(): numerator, denominator = lax.psum((numerator, denominator), 'win')  25.4 us
    all_gather x1, waiting for transfers between devices, local(): ref_sum = jnp.sum(lax.all_gather(running, 'win'), axis=0)  24.1 us
    another operation x2, other arithmetic  14.2 us
    reduce_sum x1, other arithmetic, whiten(): power_mean = jnp.mean(spectra_f * spectra_f, axis=-1, keepdims=True)  8.1 us
  transfers between devices with their start and end apart: 4, of which 4 were waited for; matrix products, arithmetic and copies ran while one was open for 7% of the time, Pallas kernels for 0%

profile of v1, /device:TPU:0, one launch (start us, length us, event | category | flops | bytes accessed | tf_op | source)
XLA Modules:
  0.0 359.4 jit_solution(1434552448215055625)
XLA Ops:
  7.2 0.0 copy-start.4
  7.2 0.0 copy-start.3
  7.2 0.0 all-gather.3.cloned.1.call-start
  7.2 0.0 copy-start
  7.2 8.1 %fusion = f32[320,8]{0,1:T(8,128)S(1)} fusion(bf16[320,8,1024]{2,1,0:T(8,128)(2,1)} %param.7), kind=kLoop, calls=%fused_computation.3 | loop fusion | flops 7861760 | bytes 5253120 | tf_op jit(solution)/shard_map/reduce_sum | solution.py:22
  15.4 0.0 copy-done
  15.4 4.2 %fusion.1 = bf16[320,8,1024]{2,0,1:T(8,128)(2,1)S(1)} fusion(f32[320,8]{0,1:T(8,128)S(1)} %add_rsqrt_fusion, bf16[320,8,1024]{2,1,0:T(8,128)(2,1)S(1)} %copy-done), kind=kLoop, calls=%fused_computation.4 | loop fusion | flops 7864320 | bytes 10496000 | tf_op jit(solution)/shard_map/convert_element_type | solution.py:23
  19.5 3.1 collective-permute-start
  22.6 2.3 collective-permute-start.1
  24.9 0.0 copy-done.4
  24.9 1.1 fusion.31
  26.1 0.0 copy-done.3
  26.1 0.0 copy-start.2
  26.1 8.2 %convert_convert_fusion = f32[512,8,1024]{2,0,1:T(8,128)} fusion(bf16[320,8,1024]{2,0,1:T(8,128)(2,1)S(1)} %fusion.1, s32[512]{0:T(512)S(1)} %copy-done.3), kind=kOutput, calls=%fused_computation.11 | convolution fusion | flops 2692907008 | bytes 22022144 | tf_op jit(solution)/shard_map/sc,cwf->swf/dot_general | solution.py:67
  34.3 0.0 copy-done.2
  34.3 8.2 %fusion.16 = f32[512,8,1024]{2,0,1:T(8,128)} fusion(bf16[320,8,1024]{2,0,1:T(8,128)(2,1)S(1)} %fusion.1, s32[512]{0:T(512)S(1)} %copy-done.2, pred[512]{0:T(512)(128)(4,1)S(1)} %get-tuple-element.17), kind=kOutput, calls=%fused_computation.26 | convolution fusion | flops 2684682240 | bytes 22022656 | tf_op jit(solution)/shard_map/sc,cwf->swf/dot_general | solution.py:67
  42.5 96.0 %collective-permute-done = bf16[320,8,1024]{2,0,1:T(8,128)(2,1)S(1)} collective-permute-done((bf16[320,8,1024]{2,0,1:T(8,128)(2,1)S(1)}, bf16[320,8,1024]{2,0,1:T(8,128)(2,1)S(1)}, u32[]{:S(2)}, u32[]{:S(2)}) %collective-permute-start) | collective-permute-done | bytes 5242912 | tf_op jit(solution)/shard_map/ppermute | solution.py:15
  138.6 8.2 %fusion.19 = f32[512,8,1024]{2,0,1:T(8,128)} fusion(bf16[320,8,1024]{2,0,1:T(8,128)(2,1)S(1)} %collective-permute-done, s32[512]{0:T(512)S(1)} %copy-done.2, pred[512]{0:T(512)(128)(4,1)S(1)} %get-tuple-element.18), kind=kOutput, calls=%fused_computation.28 | convolution fusion | flops 2684682240 | bytes 22022656 | tf_op jit(solution)/shard_map/sc,cwf->swf/dot_general | solution.py:67
  146.7 102.7 %collective-permute-done.1 = bf16[320,8,1024]{2,0,1:T(8,128)(2,1)S(1)} collective-permute-done((bf16[320,8,1024]{2,0,1:T(8,128)(2,1)S(1)}, bf16[320,8,1024]{2,0,1:T(8,128)(2,1)S(1)}, u32[]{:S(2)}, u32[]{:S(2)}) %collective-permute-start.1) | collective-permute-done | bytes 5242912 | tf_op jit(solution)/shard_map/ppermute | solution.py:16
  249.5 0.0 copy-start.1
  249.5 2.4 copy-done.1
  251.9 20.8 %fusion.6 = f32[512,8,1024]{2,0,1:T(8,128)} fusion(bf16[320,8,1024]{2,0,1:T(8,128)(2,1)} %copy-done.1, f32[512,8,1024]{2,0,1:T(8,128)} %fusion.16, f32[512,8,1024]{2,0,1:T(8,128)} %fusion.19, s32[512]{0:T(512)S(1)} %copy-done.2, pred[512]{0:T(512)(128)(4,1)S(1)} %get-tuple-element.16), kind=kOutput, calls=%fused_computation.12 | convolution fusion | flops 2701459456 | bytes 55577088 | tf_op jit(solution)/shard_map/sc,cwf->swf/dot_general | solution.py:67
  272.6 13.0 %add_convert_fusion.1 = (bf16[512,8,512]{2,0,1:T(8,128)(2,1)S(1)}, bf16[512,8,512]{2,0,1:T(8,128)(2,1)S(1)}) fusion(f32[512,8,1024]{2,0,1:T(8,128)} %fusion.6, f32[512,8,1024]{2,0,1:T(8,128)} %convert_convert_fusion), kind=kLoop, calls=%fused_computation.10 | loop fusion | flops 16777216 | bytes 41943040 | tf_op jit(solution)/shard_map/convert.2
  285.7 0.0 copy-start.5
  285.7 0.0 copy-start.6
  285.7 3.7 %fusion.39 = (f32[512,128]{0,1:T(8,128)}, bf16[512,8,128]{0,2,1:T(8,128)(2,1)S(1)}) fusion(bf16[512,128]{0,1:T(8,128)(2,1)S(1)} %get-tuple-element.15, bf16[512,128]{0,1:T(8,128)(2,1)S(1)} %get-tuple-element.14, bf16[512,8,512]{2,0,1:T(8,128)(2,1)S(1)} %get-tuple-element.11, bf16[512,8,512]{2,0,1:T(8,128)(2,1)S(1)} %get-tuple-element.10), kind=kOutput, calls=%fused_computation.63 | convolution fusion | flops 1092026368 | bytes 9961472 | tf_op jit(solution)/shard_map/dot_general | solution.py:89
  289.5 0.0 all-gather.3.cloned.1.call-update
  289.5 0.0 all-reduce.2.cloned.1.call-start
  290.2 0.0 copy-done.5
  290.2 0.0 copy-done.6
  290.2 0.2 select_reduce_fusion
  290.4 24.1 %all-gather.3.cloned.1.call-done = f32[2048,128]{0,1:T(8,128)} async-done(((f32[512,128]{0,1:T(8,128)}), f32[2048,128]{0,1:T(8,128)}) %all-gather.3.cloned.1.call-update) | async-done | bytes 1048592 | tf_op jit(solution)/shard_map/all_gather | solution.py:96
  314.5 1.9 reshape.80
  316.5 0.6 reduce_sum.83
  317.1 0.4 fusion.7
  317.5 0.1 multiply_reduce_fusion
  317.6 0.1 fusion.38
  317.7 0.9 fusion.9
  318.6 0.0 all-reduce.2.cloned.1.call-update
  318.6 0.8 copy.15
  319.4 5.9 %psum.15 = f32[512]{0:T(512)S(1)} all-reduce(f32[512]{0:T(512)S(1)} %get-tuple-element.8), channel_id=1, replica_groups=mesh['days'=2,'chan'=4,'win'=4] {'win'}, use_global_device_ids=true, to_apply=%region_10.11 | all-reduce | flops 512 | bytes 4096 | tf_op jit(solution)/shard_map/psum | solution.py:103
  325.3 25.4 %all-reduce.2.cloned.1.call-done = f32[512,128]{0,1:T(8,128)} async-done(((f32[512,128]{0,1:T(8,128)}), f32[512,128]{0,1:T(8,128)}) %all-reduce.2.cloned.1.call-update) | async-done | bytes 262160 | tf_op jit(solution)/shard_map/psum | solution.py:103
  350.7 1.0 divide_select_fusion
  351.7 0.8 copy.16
  (6 shorter events, 0.0 us)
Async XLA Ops:
  7.2 17.7 %copy-start.4 = (s32[512]{0:T(512)S(1)}, s32[512]{0:T(512)}, u32[]{:S(2)}) copy-start(s32[512]{0:T(512)} %param.9) | copy-start | bytes 6148
  7.2 18.9 %copy-start.3 = (s32[512]{0:T(512)S(1)}, s32[512]{0:T(512)}, u32[]{:S(2)}) copy-start(s32[512]{0:T(512)} %param.8) | copy-start | bytes 6148
  7.2 307.4 %all-gather.3.cloned.1.call-start = ((), (), s32[]{:S(2)}) async-start(), calls=%async_computation.1 | async-start | bytes 1310720 | tf_op jit(solution)/shard_map/all_gather | solution.py:96
  7.2 8.1 %copy-start = (bf16[320,8,1024]{2,1,0:T(8,128)(2,1)S(1)}, bf16[320,8,1024]{2,1,0:T(8,128)(2,1)}, u32[]{:S(2)}) copy-start(bf16[320,8,1024]{2,1,0:T(8,128)(2,1)} %param.7) | copy-start | bytes 15728644
  19.5 119.0 %collective-permute-start = (bf16[320,8,1024]{2,0,1:T(8,128)(2,1)S(1)}, bf16[320,8,1024]{2,0,1:T(8,128)(2,1)S(1)}, u32[]{:S(2)}, u32[]{:S(2)}) collective-permute-start(bf16[320,8,1024]{2,0,1:T(8,128)(2,1)S(1)} %fusion.1), channel_id=1, source_target_pairs={{0,4},{4,8},{8,12},{12,0},{1,5},{5,9},{9,13},{13,1},{2,6},{6,10},{... | collective-permute-start | bytes 15728648 | tf_op jit(solution)/shard_map/ppermute | solution.py:15
  22.6 226.9 %collective-permute-start.1 = (bf16[320,8,1024]{2,0,1:T(8,128)(2,1)S(1)}, bf16[320,8,1024]{2,0,1:T(8,128)(2,1)S(1)}, u32[]{:S(2)}, u32[]{:S(2)}) collective-permute-start(bf16[320,8,1024]{2,0,1:T(8,128)(2,1)S(1)} %fusion.1), channel_id=1, source_target_pairs={{4,0},{8,4},{12,8},{0,12},{5,1},{9,5},{13,9},{1,13},{6,2},{10,6},{... | collective-permute-start | bytes 15728648 | tf_op jit(solution)/shard_map/ppermute | solution.py:16
  26.1 8.2 %copy-start.2 = (s32[512]{0:T(512)S(1)}, s32[512]{0:T(512)}, u32[]{:S(2)}) copy-start(s32[512]{0:T(512)} %param.10) | copy-start | bytes 6148
  249.5 2.4 copy-start.1
  285.7 4.5 %copy-start.5 = (f32[8]{0:T(128)S(1)}, f32[8]{0:T(128)}, u32[]{:S(2)}) copy-start(f32[8]{0:T(128)} %param.13) | copy-start | bytes 100
  285.7 4.5 %copy-start.6 = (s32[8]{0:T(128)S(1)}, s32[8]{0:T(128)}, u32[]{:S(2)}) copy-start(s32[8]{0:T(128)} %param.12) | copy-start | bytes 100
  289.5 61.3 %all-reduce.2.cloned.1.call-start = ((), (), s32[]{:S(2)}) async-start(), calls=%async_computation | async-start | bytes 524288 | tf_op jit(solution)/shard_map/psum | solution.py:103
Sparse Core Ops, SparseCore 0:
  289.6 24.8 all-gather.2
  318.7 31.9 all-reduce.1
